TPU v7x, 32 devices: a whole 2x2x4 slice. The times are simulated.
32 devices in a mesh: ctx: 8 (over y, x, core), uly: 4 (over z).
Axes of the slice: x: 2, y: 2, z: 4, core: 2. Of those that a mesh axis runs over, the one named last changes fastest.
Arguments:
- query_states: bfloat16 [1024, 2048], P(('ctx', 'uly')), may hold values from -8 to 8
- key_states: bfloat16 [1024, 2048], P(('ctx', 'uly')), may hold values from -8 to 8
- value_states: bfloat16 [1024, 2048], P(('ctx', 'uly')), may hold values from -6 to 6
- score_kernel: float32 [16, 6, 11], P('uly'), may hold values from -0.4 to 1.2
- head_mixing: float32 [16, 4], P('uly'), may hold values from 0.25 to 1
- head_gain: float32 [2048], P('uly'), may hold values from 0.5 to 1.5
Outputs:
- attended: bfloat16 [1024, 2048], P(('ctx', 'uly'))
All inputs are finite; a program needn't handle non-finite values.
Results may differ from a plain program's by a relative error of at most 0.0049.
Values may be sent and summed in bfloat16 or wider, within the bound.
No kernel may reach another device: no remote copies, remote signals or barrier semaphores. Data moves between devices by JAX's collectives and lax.ppermute only.
A program may use at most 64 MiB of HBM per device.

v0:
```python
import jax
import jax.numpy as jnp
from jax import lax
from jax.sharding import PartitionSpec as P

GROUP = 4
QCONV = 6
KCONV = 11
KEY_BLOCK = 128
ROW_CHUNK = 128
KEY_GROUP = 8
lowest = -1e30
epsilon = 1e-06


def passed_along(shard, axis, by):
    peers = lax.axis_size(axis)
    pairs = [(i, i + by) for i in range(peers) if 0 <= i + by < peers]
    return lax.ppermute(shard, axis, pairs)


def split_bf16(values):
    high = lax.reduce_precision(values, exponent_bits=8, mantissa_bits=7)
    low = values - high
    return (high.astype(jnp.bfloat16), low.astype(jnp.bfloat16))


def toeplitz_terms(score_kernel, head_dim):
    col_lead = KCONV - 1
    scaled = score_kernel * head_dim ** (-0.5)
    lag = (
        lax.iota(jnp.int32, KEY_BLOCK)[:, None]
        + col_lead
        - lax.iota(jnp.int32, KEY_BLOCK + col_lead)[None, :]
    )
    toeplitz = jnp.zeros(score_kernel.shape[:2] + lag.shape, jnp.float32)
    for col_lag in range(KCONV):
        toeplitz = jnp.where(lag == col_lag, scaled[:, :, col_lag, None, None], toeplitz)
    return split_bf16(toeplitz)


def convolved_keys(key_windows, terms):
    high, low = terms
    heads = high.shape[0]
    key_heads = key_windows.reshape(key_windows.shape[:2] + (heads, -1))
    conv_keys = jnp.einsum(
        "harc,nchd->nhard", high, key_heads, preferred_element_type=jnp.float32
    ) + jnp.einsum("harc,nchd->nhard", low, key_heads, preferred_element_type=jnp.float32)
    return split_bf16(conv_keys)


def band_terms(query_rows, query_first, key_flat, score_kernel):
    row_lead = QCONV - 1
    heads = score_kernel.shape[0]
    ext_count = query_rows.shape[0]
    row_count = ext_count - row_lead
    near = lax.dynamic_slice_in_dim(key_flat, query_first + 4, ext_count + QCONV - 2, 0)
    query_heads = query_rows.reshape(ext_count, heads, -1).astype(jnp.float32)
    near_heads = near.reshape(near.shape[0], heads, -1).astype(jnp.float32)
    scale = query_heads.shape[2] ** (-0.5)
    diagonals = [
        jnp.sum(query_heads * near_heads[lag - 1 : lag - 1 + ext_count], axis=2) * scale
        for lag in range(1, QCONV)
    ]
    band = []
    for gap in range(QCONV - 1):
        acc = jnp.zeros((row_count, heads), jnp.float32)
        for row_lag in range(gap + 1, QCONV):
            for col_lag in range(row_lag - gap):
                lag = row_lag - col_lag - gap
                acc = (
                    acc
                    - score_kernel[None, :, row_lag, col_lag]
                    * diagonals[lag - 1][row_lead - row_lag : row_lead - row_lag + row_count]
                )
        band.append(acc.T)
    return jnp.stack(band)


def group_logits(shifted, key_windows, terms):
    keys_high, keys_low = convolved_keys(key_windows, terms)
    return jnp.einsum(
        "ihad,nhard->hinr", shifted, keys_high, preferred_element_type=jnp.float32
    ) + jnp.einsum("ihad,nhard->hinr", shifted, keys_low, preferred_element_type=jnp.float32)


def attend_chunk(shifted, band, query_first, key_windows, terms, value_heads, head_mixing):
    row_count, heads = shifted.shape[:2]
    seq_len = value_heads.shape[0]
    window_count = key_windows.shape[0]
    if window_count <= KEY_GROUP:
        convolved = group_logits(shifted, key_windows, terms)
    else:
        grouped_windows = key_windows.reshape(
            (window_count // KEY_GROUP, KEY_GROUP) + key_windows.shape[1:]
        )
        convolved = lax.map(lambda windows: group_logits(shifted, windows, terms), grouped_windows)
        convolved = jnp.moveaxis(convolved, 0, 2)
    convolved = convolved.reshape(heads, row_count, seq_len)
    query_pos = query_first + lax.iota(jnp.int32, row_count)
    gap = query_pos[:, None] - lax.iota(jnp.int32, seq_len)[None, :]
    for lag in range(QCONV - 1):
        convolved = convolved + jnp.where(gap == lag, band[lag][:, :, None], 0.0)
    logits = jnp.where(gap >= 0, convolved, lowest)
    peak = jnp.max(logits, axis=2, keepdims=True)
    expd = jnp.exp(logits - peak)
    probabilities = expd / jnp.sum(expd, axis=2, keepdims=True)
    grouped = probabilities.reshape(heads // GROUP, GROUP, row_count, seq_len)
    weights = head_mixing.reshape(heads // GROUP, GROUP, GROUP)
    mixed_probs = jnp.zeros_like(grouped)
    for source in range(GROUP):
        mixed_probs = mixed_probs + weights[:, :, source, None, None] * grouped[:, source, None]
    mixed_probs = mixed_probs.reshape(heads, row_count, seq_len).astype(jnp.bfloat16)
    return jnp.einsum("hik,khd->ihd", mixed_probs, value_heads, preferred_element_type=jnp.float32)


def normalize(weighted, gain_local):
    factor = lax.rsqrt(jnp.mean(weighted * weighted, axis=2, keepdims=True) + epsilon)
    return (
        (weighted * factor * gain_local[None]).astype(jnp.bfloat16).reshape(weighted.shape[0], -1)
    )


def shards(query_states, key_states, value_states, score_kernel, head_mixing, head_gain):
    stacked = jnp.stack([query_states, key_states, value_states])
    query_local, key_local, value_local = lax.all_to_all(
        stacked, "uly", split_axis=2, concat_axis=1, tiled=True
    )
    shard_rows = query_local.shape[0]
    width = query_local.shape[1]
    row_lead = QCONV - 1
    col_lead = KCONV - 1
    heads = score_kernel.shape[0]
    head_dim = width // heads
    ctx_place = lax.axis_index("ctx")
    query_first = ctx_place * shard_rows
    earlier = passed_along(query_local[shard_rows - row_lead :], "ctx", 1)
    query_ext = jnp.concatenate([earlier, query_local], axis=0)
    key_all, value_all = lax.all_gather(
        jnp.stack([key_local, value_local]), "ctx", axis=1, tiled=True
    )
    seq_len = key_all.shape[0]
    key_pad = jnp.concatenate([jnp.zeros((col_lead, width), key_all.dtype), key_all], axis=0)
    key_windows = jnp.stack(
        [key_pad[start : start + KEY_BLOCK + col_lead] for start in range(0, seq_len, KEY_BLOCK)]
    )
    terms = toeplitz_terms(score_kernel, head_dim)
    edge = jnp.zeros((8, width), key_all.dtype)
    key_flat = jnp.concatenate([edge, key_all, edge], axis=0)
    band = band_terms(query_ext, query_first, key_flat, score_kernel)
    query_heads = query_ext.reshape(shard_rows + row_lead, heads, head_dim)
    shifted = jnp.stack(
        [query_heads[row_lead - lag : row_lead - lag + shard_rows] for lag in range(QCONV)], axis=2
    )
    value_heads = value_all.reshape(seq_len, heads, head_dim)
    chunk = min(ROW_CHUNK * KEY_BLOCK * 8 // seq_len, shard_rows)
    if chunk == shard_rows:
        weighted = attend_chunk(
            shifted, band, query_first, key_windows, terms, value_heads, head_mixing
        )
    else:
        chunks = shard_rows // chunk

        def one_chunk(index):
            start = index * chunk
            return attend_chunk(
                lax.dynamic_slice_in_dim(shifted, start, chunk, 0),
                lax.dynamic_slice_in_dim(band, start, chunk, 2),
                query_first + start,
                key_windows,
                terms,
                value_heads,
                head_mixing,
            )

        weighted = lax.map(one_chunk, jnp.arange(chunks, dtype=jnp.int32))
        weighted = weighted.reshape((shard_rows,) + weighted.shape[2:])
    gain_local = head_gain.reshape(heads, head_dim)
    attended = normalize(weighted, gain_local)
    return lax.all_to_all(attended, "uly", split_axis=0, concat_axis=1, tiled=True)


def solution(mesh):
    placed = (
        P(("ctx", "uly"), None),
        P(("ctx", "uly"), None),
        P(("ctx", "uly"), None),
        P("uly", None, None),
        P("uly", None),
        P("uly"),
    )
    return jax.shard_map(
        shards, mesh=mesh, in_specs=placed, out_specs=P(("ctx", "uly"), None), check_vma=False
    )
```

profile of v0, /device:TPU:0, one launch (start us, length us, event | category | flops | bytes accessed | tf_op | source)
XLA Modules:
  0.0 156.9 jit_solution(3671239521716522393)
XLA Ops:
  6.5 1.1 pad_maximum_fusion
  7.6 1.4 copy.223
  9.0 1.6 %reshape.295 = bf16[4,2,24576]{2,1,0:T(2,128)(2,1)S(1)} reshape(bf16[2048,3,32]{2,1,0:T(4,128)(2,1)S(1)} %bitcast.118) | data formatting | bytes 786432
  10.6 17.8 %all_to_all.34 = bf16[4,2,24576]{2,1,0:T(2,128)(2,1)S(1)} all-to-all(bf16[4,2,24576]{2,1,0:T(2,128)(2,1)S(1)} %reshape.295), channel_id=1, replica_groups=mesh['ctx'=8,'uly'=4] {'uly'}, dimensions={0} | all-to-all | bytes 786432 | tf_op jit(solution)/shard_map/all_to_all | solution.py:126
  28.4 1.3 reshape.296
  29.7 1.2 copy.282
  30.9 0.1 fusion.128
  31.1 0.8 pad_maximum_fusion.1
  32.5 0.7 copy.255
  33.2 0.6 copy.254
  33.8 0.7 copy.253
  34.5 0.7 copy.252
  35.2 0.7 copy.251
  35.9 0.7 copy.250
  36.5 0.7 copy.249
  37.2 0.7 slice_reduce_fusion.18
  38.0 1.0 slice_reduce_fusion.17
  39.0 0.8 fusion.108
  39.7 1.2 fusion.84
  41.0 1.2 subtract_compare_fusion.5
  42.3 1.3 collective-permute-start
  43.6 0.7 concatenate.20
  45.2 0.1 copy.238
  45.7 0.1 copy.240
  45.8 0.6 concatenate.19
  46.6 12.5 %all-gather.2.cloned.1.call-done = bf16[2,1024,512]{2,1,0:T(8,128)(2,1)} async-done(((bf16[2,128,512]{2,1,0:T(8,128)(2,1)}), bf16[2,1024,512]{2,1,0:T(8,128)(2,1)}) %all-gather.2.cloned.1.call-update) | async-done | bytes 2097168 | tf_op jit(solution)/shard_map/all_gather | solution.py:139
  59.1 1.7 %slice_bitcast_fusion = (bf16[1024,512]{1,0:T(8,128)(2,1)S(1)}, bf16[1,1024,512]{2,1,0:T(8,128)(2,1)S(1)}) fusion(bf16[2,1024,512]{2,1,0:T(8,128)(2,1)} %all-gather.2.cloned.1.call-done), kind=kLoop, calls=%fused_computation.39 | loop fusion | bytes 4194304 | tf_op jit(solution)/shard_map/unstack | solution.py:139
  60.8 0.7 pad_slice_fusion
  61.5 1.6 %stack.75 = bf16[1,138,4,128]{3,2,1,0:T(4,128)(2,1)} reshape(bf16[138,512]{1,0:T(8,128)(2,1)} %pad_slice_fusion) | data formatting | bytes 282624 | tf_op jit(solution)/shard_map/stack | solution.py:144
  63.1 1.6 %copy_dynamic-update-slice_fusion.7 = bf16[8,138,4,128]{3,1,0,2:T(8,128)(2,1)} fusion(bf16[1,138,4,128]{3,2,1,0:T(4,128)(2,1)} %stack.75), kind=kLoop, calls=%fused_computation.138 | loop fusion | bytes 288768
  64.7 2.4 %fusion.127 = (bf16[1,138,512]{2,1,0:T(8,128)(2,1)}, bf16[1,138,512]{2,1,0:T(8,128)(2,1)}, bf16[1,138,512]{2,1,0:T(8,128)(2,1)}, bf16[1,138,512]{2,1,0:T(8,128)(...) fusion(bf16[2,1024,512]{2,1,0:T(8,128)(2,1)} %all-gather.2.cloned.1.call-done), kind=kLoop, calls=%fused_computation.217 | loop fusion | bytes 1978368 | tf_op jit(solution)/shard_map/slice | solution.py:145
  67.1 1.6 %stack.76 = bf16[1,138,4,128]{3,2,1,0:T(4,128)(2,1)} reshape(bf16[1,138,512]{2,1,0:T(8,128)(2,1)} %get-tuple-element.39) | data formatting | bytes 282624 | tf_op jit(solution)/shard_map/stack | solution.py:144
  68.7 1.6 %stack.77 = bf16[1,138,4,128]{3,2,1,0:T(4,128)(2,1)} reshape(bf16[1,138,512]{2,1,0:T(8,128)(2,1)} %get-tuple-element.38) | data formatting | bytes 282624 | tf_op jit(solution)/shard_map/stack | solution.py:144
  70.3 1.6 %stack.78 = bf16[1,138,4,128]{3,2,1,0:T(4,128)(2,1)} reshape(bf16[1,138,512]{2,1,0:T(8,128)(2,1)} %get-tuple-element.37) | data formatting | bytes 282624 | tf_op jit(solution)/shard_map/stack | solution.py:144
  71.9 1.6 %stack.79 = bf16[1,138,4,128]{3,2,1,0:T(4,128)(2,1)} reshape(bf16[1,138,512]{2,1,0:T(8,128)(2,1)} %get-tuple-element.36) | data formatting | bytes 282624 | tf_op jit(solution)/shard_map/stack | solution.py:144
  73.5 1.6 %stack.80 = bf16[1,138,4,128]{3,2,1,0:T(4,128)(2,1)} reshape(bf16[1,138,512]{2,1,0:T(8,128)(2,1)} %get-tuple-element.35) | data formatting | bytes 282624 | tf_op jit(solution)/shard_map/stack | solution.py:144
  75.1 1.6 %stack.81 = bf16[1,138,4,128]{3,2,1,0:T(4,128)(2,1)} reshape(bf16[1,138,512]{2,1,0:T(8,128)(2,1)} %get-tuple-element.34) | data formatting | bytes 282624 | tf_op jit(solution)/shard_map/stack | solution.py:144
  76.7 1.6 %stack.82 = bf16[1,138,4,128]{3,2,1,0:T(4,128)(2,1)} reshape(bf16[1,138,512]{2,1,0:T(8,128)(2,1)} %get-tuple-element.33) | data formatting | bytes 282624 | tf_op jit(solution)/shard_map/stack | solution.py:144
  78.3 1.6 %copy_dynamic-update-slice_fusion.6 = bf16[8,138,4,128]{3,1,0,2:T(8,128)(2,1)} fusion(bf16[8,138,4,128]{3,1,0,2:T(8,128)(2,1)} %copy_dynamic-update-slice_fusion.7, bf16[1,138,4,128]{3,2,1,0:T(4,128)(2,1)} %stack.76), kind=kLoop, calls=%fused_computation.137 | loop fusion | bytes 288768
  79.9 1.6 %copy_dynamic-update-slice_fusion.5 = bf16[8,138,4,128]{3,1,0,2:T(8,128)(2,1)} fusion(bf16[8,138,4,128]{3,1,0,2:T(8,128)(2,1)} %copy_dynamic-update-slice_fusion.6, bf16[1,138,4,128]{3,2,1,0:T(4,128)(2,1)} %stack.77), kind=kLoop, calls=%fused_computation.136 | loop fusion | bytes 288768
  81.5 1.6 %copy_dynamic-update-slice_fusion.4 = bf16[8,138,4,128]{3,1,0,2:T(8,128)(2,1)} fusion(bf16[8,138,4,128]{3,1,0,2:T(8,128)(2,1)} %copy_dynamic-update-slice_fusion.5, bf16[1,138,4,128]{3,2,1,0:T(4,128)(2,1)} %stack.78), kind=kLoop, calls=%fused_computation.135 | loop fusion | bytes 288768
  83.1 1.6 %copy_dynamic-update-slice_fusion.3 = bf16[8,138,4,128]{3,1,0,2:T(8,128)(2,1)} fusion(bf16[8,138,4,128]{3,1,0,2:T(8,128)(2,1)} %copy_dynamic-update-slice_fusion.4, bf16[1,138,4,128]{3,2,1,0:T(4,128)(2,1)} %stack.79), kind=kLoop, calls=%fused_computation.134 | loop fusion | bytes 288768
  84.7 1.6 %copy_dynamic-update-slice_fusion.2 = bf16[8,138,4,128]{3,1,0,2:T(8,128)(2,1)} fusion(bf16[8,138,4,128]{3,1,0,2:T(8,128)(2,1)} %copy_dynamic-update-slice_fusion.3, bf16[1,138,4,128]{3,2,1,0:T(4,128)(2,1)} %stack.80), kind=kLoop, calls=%fused_computation.133 | loop fusion | bytes 288768
  86.3 1.6 %copy_dynamic-update-slice_fusion.1 = bf16[8,138,4,128]{3,1,0,2:T(8,128)(2,1)} fusion(bf16[8,138,4,128]{3,1,0,2:T(8,128)(2,1)} %copy_dynamic-update-slice_fusion.2, bf16[1,138,4,128]{3,2,1,0:T(4,128)(2,1)} %stack.81), kind=kLoop, calls=%fused_computation.132 | loop fusion | bytes 288768
  87.9 1.6 %copy_dynamic-update-slice_fusion = bf16[8,138,4,128]{3,1,0,2:T(8,128)(2,1)} fusion(bf16[8,138,4,128]{3,1,0,2:T(8,128)(2,1)} %copy_dynamic-update-slice_fusion.1, bf16[1,138,4,128]{3,2,1,0:T(4,128)(2,1)} %stack.82), kind=kLoop, calls=%fused_computation.131 | loop fusion | bytes 288768 | tf_op jit(solution)/shard_map/stack | solution.py:144
  89.6 8.7 %fusion.17 = f32[4,8,128,6,128]{4,2,3,1,0:T(8,128)} fusion(bf16[8,138,4,128]{3,1,0,2:T(8,128)(2,1)} %copy_dynamic-update-slice_fusion, f32[4,6]{1,0:T(4,128)S(1)} %bitcast.135, f32[4,6]{1,0:T(4,128)S(1)} %bitcast.137, f32[4,6]{1,0:T(4,128)S(1)} %bitcast.139, f32[4,6]{1,0:T(4,128)S(1)} %bitcast.141, f32[4,6]{1,0:T(4,128)} %bitcast.143, ...), kind=kOutput, calls=%fused_computation.32 | convolution fusion | flops 873732096 | bytes 13908768 | tf_op jit(solution)/shard_map/harc,nchd->nhard/dot_general | solution.py:46
  98.5 6.3 %fusion.15 = f32[4,8,128,6,128]{4,2,3,1,0:T(8,128)} fusion(bf16[8,138,4,128]{3,1,0,2:T(8,128)(2,1)S(1)} %copy-done, f32[4,6]{1,0:T(4,128)S(1)} %bitcast.136, f32[4,6]{1,0:T(4,128)S(1)} %bitcast.138, f32[4,6]{1,0:T(4,128)S(1)} %bitcast.140, f32[4,6]{1,0:T(4,128)S(1)} %bitcast.142, f32[4,6]{1,0:T(4,128)S(1)} %bitcast.144, f32[4,6]{1,0:T(4,128)S(1)} %bitcast.146, ...), kind=kOutput, calls=%fused_computation.30 | convolution fusion | flops 874156032 | bytes 13908768 | tf_op jit(solution)/shard_map/harc,nchd->nhard/dot_general | solution.py:48
  104.8 1.4 copy.227
  106.3 0.1 fusion.129
  107.0 0.2 copy-done.5
  107.2 0.8 fusion.90
  108.6 10.9 %fusion.1 = f32[4,128,8,128,1]{1,3,4,2,0:T(8,128)S(1)} fusion(f32[4,8,128,6,128]{4,2,3,1,0:T(8,128)} %fusion.17, f32[4,8,128,6,128]{4,2,3,1,0:T(8,128)} %fusion.15, bf16[128,4,6,128]{3,0,2,1:T(8,128)(2,1)S(1)} %constant_dynamic-update-slice_fusion), kind=kOutput, calls=%fused_computation.3 | convolution fusion | flops 817889280 | bytes 28049408 | tf_op jit(solution)/shard_map/ihad,nhard->hinr/dot_general | solution.py:84
  119.9 10.4 %fusion.85 = (f32[4,128]{1,0:T(4,128)S(1)}, f32[4,128,8,128]{1,3,2,0:T(8,128)S(1)}) fusion(f32[4,128]{1,0:T(4,128)S(1)} %get-tuple-element.74, pred[128,8,128]{0,2,1:T(8,128)(4,1)S(1)} %get-tuple-element.69, f32[4,128]{1,0:T(4,128)S(1)} %get-tuple-element.67, pred[128,8,128]{0,2,1:T(8,128)(4,1)S(1)} %get-tuple-element.70, ...), kind=kOutput, calls=%fused_computation.115 | convolution fusion | flops 821558784 | bytes 30945280 | tf_op jit(solution)/shard_map/ihad,nhard->hinr/dot_general | solution.py:82
  130.4 1.3 exponential_reduce_fusion
  131.7 1.3 fusion.13
  133.0 0.1 slice_bitcast_fusion.4
  133.1 1.0 copy.271
  134.1 1.0 copy.270
  135.2 1.0 copy.269
  136.2 0.2 copy.268
  136.5 1.8 %multiply_reduce_fusion = (f32[128,4]{0,1:T(4,128)S(1)}, f32[128,4,128]{0,2,1:T(8,128)S(1)}) fusion(bf16[1024,4,128]{0,2,1:T(8,128)(2,1)S(1)} %bitcast.123, f32[128,1024]{1,0:T(8,128)S(1)} %copy-done.3, f32[4]{0:T(128)S(1)} %copy-done.50, f32[128,1024]{1,0:T(8,128)S(1)} %copy-done.4, f32[4]{0:T(128)S(1)} %copy-done.51, f32[128,1024]{1,0:T(8,128)} %copy.269, ...), kind=kOutput, calls=%fused_computation.127 | convolution fusion | flops 138542592 | bytes 3409984 | tf_op jit(solution)/shard_map/hik,khd->ihd/dot_general | solution.py:114
  138.5 0.1 copy.272
  138.7 10.7 %all_to_all.35 = bf16[4,32,512]{2,1,0:T(8,128)(2,1)S(1)} all-to-all(bf16[4,32,512]{2,1,0:T(8,128)(2,1)S(1)} %all_to_all.28), channel_id=1, replica_groups=mesh['ctx'=8,'uly'=4] {'uly'}, dimensions={0} | all-to-all | bytes 262144 | tf_op jit(solution)/shard_map/all_to_all | solution.py:180
  149.4 0.7 copy.284
  (158 shorter events, 3.8 us)
Async XLA Ops:
  6.5 52.5 %all-gather.2.cloned.1.call-start = ((), (), s32[]{:S(2)}) async-start(), calls=%async_computation.2 | async-start | bytes 2359296 | tf_op jit(solution)/shard_map/all_gather | solution.py:139
  29.7 2.2 %copy-start.23 = (f32[4,6,11]{2,0,1:T(4,128)S(1)}, f32[4,6,11]{2,0,1:T(4,128)}, u32[]{:S(2)}) copy-start(f32[4,6,11]{2,0,1:T(4,128)} %param.9) | copy-start | bytes 3172
  29.7 7.5 %copy-start.31 = (f32[4,4]{1,0:T(4,128)S(1)}, f32[4,4]{1,0:T(4,128)}, u32[]{:S(2)}) copy-start(f32[4,4]{1,0:T(4,128)} %param.10) | copy-start | bytes 196
  42.3 2.1 %collective-permute-start = (bf16[5,512]{1,0:T(8,128)(2,1)S(1)}, bf16[5,512]{1,0:T(8,128)(2,1)S(1)}, u32[]{:S(2)}, u32[]{:S(2)}) collective-permute-start(bf16[5,512]{1,0:T(8,128)(2,1)S(1)} %slice.356), channel_id=1, source_target_pairs={{0,4},{4,8},{8,12},{12,16},{16,20},{20,24},{24,28},{1,5},{5,9},{9,... | collective-permute-start | bytes 15368 | tf_op jit(solution)/shard_map/ppermute | solution.py:19
  89.5 8.9 %copy-start = (bf16[8,138,4,128]{3,1,0,2:T(8,128)(2,1)S(1)}, bf16[8,138,4,128]{3,1,0,2:T(8,128)(2,1)}, u32[]{:S(2)}) copy-start(bf16[8,138,4,128]{3,1,0,2:T(8,128)(2,1)} %copy_dynamic-update-slice_fusion) | copy-start | bytes 3391492
  89.5 8.9 %copy-start.12 = (pred[128,138]{0,1:T(8,128)(4,1)S(1)}, pred[128,138]{0,1:T(8,128)(4,1)}, u32[]{:S(2)}) copy-start(pred[128,138]{0,1:T(8,128)(4,1)} %get-tuple-element.81) | copy-start | bytes 52996
  89.5 8.9 %copy-start.13 = (pred[128,138]{0,1:T(8,128)(4,1)S(1)}, pred[128,138]{0,1:T(8,128)(4,1)}, u32[]{:S(2)}) copy-start(pred[128,138]{0,1:T(8,128)(4,1)} %get-tuple-element.82) | copy-start | bytes 52996
  89.5 8.9 %copy-start.14 = (pred[128,138]{0,1:T(8,128)(4,1)S(1)}, pred[128,138]{0,1:T(8,128)(4,1)}, u32[]{:S(2)}) copy-start(pred[128,138]{0,1:T(8,128)(4,1)} %get-tuple-element.83) | copy-start | bytes 52996
  89.5 8.9 %copy-start.15 = (pred[128,138]{0,1:T(8,128)(4,1)S(1)}, pred[128,138]{0,1:T(8,128)(4,1)}, u32[]{:S(2)}) copy-start(pred[128,138]{0,1:T(8,128)(4,1)} %get-tuple-element.84) | copy-start | bytes 52996
  89.5 8.9 %copy-start.16 = (pred[128,138]{0,1:T(8,128)(4,1)S(1)}, pred[128,138]{0,1:T(8,128)(4,1)}, u32[]{:S(2)}) copy-start(pred[128,138]{0,1:T(8,128)(4,1)} %get-tuple-element.85) | copy-start | bytes 52996
  89.5 8.9 %copy-start.17 = (pred[128,138]{0,1:T(8,128)(4,1)S(1)}, pred[128,138]{0,1:T(8,128)(4,1)}, u32[]{:S(2)}) copy-start(pred[128,138]{0,1:T(8,128)(4,1)} %get-tuple-element.86) | copy-start | bytes 52996
  89.5 8.9 %copy-start.18 = (pred[128,138]{0,1:T(8,128)(4,1)S(1)}, pred[128,138]{0,1:T(8,128)(4,1)}, u32[]{:S(2)}) copy-start(pred[128,138]{0,1:T(8,128)(4,1)} %get-tuple-element.87) | copy-start | bytes 52996
  89.5 8.9 %copy-start.19 = (pred[128,138]{0,1:T(8,128)(4,1)S(1)}, pred[128,138]{0,1:T(8,128)(4,1)}, u32[]{:S(2)}) copy-start(pred[128,138]{0,1:T(8,128)(4,1)} %get-tuple-element.88) | copy-start | bytes 52996
  89.5 8.9 %copy-start.20 = (pred[128,138]{0,1:T(8,128)(4,1)S(1)}, pred[128,138]{0,1:T(8,128)(4,1)}, u32[]{:S(2)}) copy-start(pred[128,138]{0,1:T(8,128)(4,1)} %get-tuple-element.89) | copy-start | bytes 52996
  89.5 8.9 %copy-start.21 = (pred[128,138]{0,1:T(8,128)(4,1)S(1)}, pred[128,138]{0,1:T(8,128)(4,1)}, u32[]{:S(2)}) copy-start(pred[128,138]{0,1:T(8,128)(4,1)} %get-tuple-element.90) | copy-start | bytes 52996
  89.6 8.9 %copy-start.22 = (pred[128,138]{0,1:T(8,128)(4,1)S(1)}, pred[128,138]{0,1:T(8,128)(4,1)}, u32[]{:S(2)}) copy-start(pred[128,138]{0,1:T(8,128)(4,1)} %get-tuple-element.91) | copy-start | bytes 52996
  89.6 8.9 %copy-start.24 = (f32[4,6,1]{1,0,2:T(4,128)S(1)}, f32[4,6,1]{1,0,2:T(4,128)}, u32[]{:S(2)}) copy-start(f32[4,6,1]{1,0,2:T(4,128)} %copy.255) | copy-start | bytes 292
  89.6 8.9 %copy-start.25 = (f32[4,6,1]{1,0,2:T(4,128)S(1)}, f32[4,6,1]{1,0,2:T(4,128)}, u32[]{:S(2)}) copy-start(f32[4,6,1]{1,0,2:T(4,128)} %copy.254) | copy-start | bytes 292
  89.6 8.9 %copy-start.26 = (f32[4,6,1]{1,0,2:T(4,128)S(1)}, f32[4,6,1]{1,0,2:T(4,128)}, u32[]{:S(2)}) copy-start(f32[4,6,1]{1,0,2:T(4,128)} %copy.253) | copy-start | bytes 292
  89.6 8.9 %copy-start.27 = (f32[4,6,1]{1,0,2:T(4,128)S(1)}, f32[4,6,1]{1,0,2:T(4,128)}, u32[]{:S(2)}) copy-start(f32[4,6,1]{1,0,2:T(4,128)} %copy.252) | copy-start | bytes 292
  89.6 8.9 %copy-start.28 = (f32[4,6,1]{1,0,2:T(4,128)S(1)}, f32[4,6,1]{1,0,2:T(4,128)}, u32[]{:S(2)}) copy-start(f32[4,6,1]{1,0,2:T(4,128)} %copy.251) | copy-start | bytes 292
  89.6 8.9 %copy-start.29 = (f32[4,6,1]{1,0,2:T(4,128)S(1)}, f32[4,6,1]{1,0,2:T(4,128)}, u32[]{:S(2)}) copy-start(f32[4,6,1]{1,0,2:T(4,128)} %copy.250) | copy-start | bytes 292
  89.6 8.9 %copy-start.30 = (f32[4,6,1]{1,0,2:T(4,128)S(1)}, f32[4,6,1]{1,0,2:T(4,128)}, u32[]{:S(2)}) copy-start(f32[4,6,1]{1,0,2:T(4,128)} %copy.249) | copy-start | bytes 292
  106.3 0.9 copy-start.5
  106.3 0.9 copy-start.32
  108.4 11.0 %copy-start.33 = (f32[4]{0:T(128)S(1)}, f32[4]{0:T(128)}, u32[]{:S(2)}) copy-start(f32[4]{0:T(128)} %get-tuple-element.11) | copy-start | bytes 52
  108.4 11.0 %copy-start.34 = (f32[4]{0:T(128)S(1)}, f32[4]{0:T(128)}, u32[]{:S(2)}) copy-start(f32[4]{0:T(128)} %get-tuple-element.12) | copy-start | bytes 52
  108.4 11.0 %copy-start.35 = (f32[4]{0:T(128)S(1)}, f32[4]{0:T(128)}, u32[]{:S(2)}) copy-start(f32[4]{0:T(128)} %get-tuple-element.13) | copy-start | bytes 52
  108.5 11.0 %copy-start.36 = (f32[4]{0:T(128)S(1)}, f32[4]{0:T(128)}, u32[]{:S(2)}) copy-start(f32[4]{0:T(128)} %get-tuple-element.16) | copy-start | bytes 52
  108.5 11.0 %copy-start.37 = (f32[4]{0:T(128)S(1)}, f32[4]{0:T(128)}, u32[]{:S(2)}) copy-start(f32[4]{0:T(128)} %get-tuple-element.17) | copy-start | bytes 52
  108.5 11.0 %copy-start.38 = (f32[4]{0:T(128)S(1)}, f32[4]{0:T(128)}, u32[]{:S(2)}) copy-start(f32[4]{0:T(128)} %get-tuple-element.20) | copy-start | bytes 52
  108.5 11.1 %copy-start.39 = (f32[4]{0:T(128)S(1)}, f32[4]{0:T(128)}, u32[]{:S(2)}) copy-start(f32[4]{0:T(128)} %get-tuple-element.15) | copy-start | bytes 52
  108.5 11.1 %copy-start.40 = (f32[4]{0:T(128)S(1)}, f32[4]{0:T(128)}, u32[]{:S(2)}) copy-start(f32[4]{0:T(128)} %get-tuple-element.19) | copy-start | bytes 52
  108.5 11.1 %copy-start.41 = (f32[4]{0:T(128)S(1)}, f32[4]{0:T(128)}, u32[]{:S(2)}) copy-start(f32[4]{0:T(128)} %get-tuple-element.22) | copy-start | bytes 52
  108.5 11.1 %copy-start.42 = (f32[4]{0:T(128)S(1)}, f32[4]{0:T(128)}, u32[]{:S(2)}) copy-start(f32[4]{0:T(128)} %get-tuple-element.24) | copy-start | bytes 52
  108.5 11.2 %copy-start.44 = (f32[4]{0:T(128)S(1)}, f32[4]{0:T(128)}, u32[]{:S(2)}) copy-start(f32[4]{0:T(128)} %get-tuple-element.10) | copy-start | bytes 52
  108.5 11.2 %copy-start.45 = (f32[4]{0:T(128)S(1)}, f32[4]{0:T(128)}, u32[]{:S(2)}) copy-start(f32[4]{0:T(128)} %get-tuple-element.14) | copy-start | bytes 52
  108.5 11.2 %copy-start.46 = (f32[4]{0:T(128)S(1)}, f32[4]{0:T(128)}, u32[]{:S(2)}) copy-start(f32[4]{0:T(128)} %get-tuple-element.18) | copy-start | bytes 52
  108.6 11.2 %copy-start.47 = (f32[4]{0:T(128)S(1)}, f32[4]{0:T(128)}, u32[]{:S(2)}) copy-start(f32[4]{0:T(128)} %get-tuple-element.21) | copy-start | bytes 52
  108.6 11.2 %copy-start.48 = (f32[4]{0:T(128)S(1)}, f32[4]{0:T(128)}, u32[]{:S(2)}) copy-start(f32[4]{0:T(128)} %get-tuple-element.23) | copy-start | bytes 52
  108.6 11.3 %copy-start.1 = (pred[128,8,128]{0,2,1:T(8,128)(4,1)S(1)}, pred[128,8,128]{0,2,1:T(8,128)(4,1)}, u32[]{:S(2)}) copy-start(pred[128,8,128]{0,2,1:T(8,128)(4,1)} %get-tuple-element.73) | copy-start | bytes 393220
  130.3 1.3 copy-start.6
  130.3 1.3 copy-start.7
  130.3 1.3 copy-start.8
  130.4 1.3 copy-start.9
  130.4 1.3 copy-start.10
  130.4 1.3 copy-start.11
  133.1 3.3 %copy-start.2 = (bf16[1,1024,512]{1,2,0:T(8,128)(2,1)S(1)}, bf16[1,1024,512]{1,2,0:T(8,128)(2,1)}, u32[]{:S(2)}) copy-start(bf16[1,1024,512]{1,2,0:T(8,128)(2,1)} %copy.227) | copy-start | bytes 3145732
  133.1 3.3 %copy-start.49 = (f32[4]{0:T(128)S(1)}, f32[4]{0:T(128)}, u32[]{:S(2)}) copy-start(f32[4]{0:T(128)} %get-tuple-element.25) | copy-start | bytes 52
  133.1 3.3 %copy-start.50 = (f32[4]{0:T(128)S(1)}, f32[4]{0:T(128)}, u32[]{:S(2)}) copy-start(f32[4]{0:T(128)} %get-tuple-element.26) | copy-start | bytes 52
  133.1 3.3 %copy-start.51 = (f32[4]{0:T(128)S(1)}, f32[4]{0:T(128)}, u32[]{:S(2)}) copy-start(f32[4]{0:T(128)} %get-tuple-element.27) | copy-start | bytes 52
  133.1 3.3 %copy-start.52 = (f32[4]{0:T(128)S(1)}, f32[4]{0:T(128)}, u32[]{:S(2)}) copy-start(f32[4]{0:T(128)} %get-tuple-element.28) | copy-start | bytes 52
  134.1 2.3 %copy-start.3 = (f32[128,1024]{1,0:T(8,128)S(1)}, f32[128,1024]{1,0:T(8,128)}, u32[]{:S(2)}) copy-start(f32[128,1024]{1,0:T(8,128)} %copy.271) | copy-start | bytes 1572868
  135.2 1.3 copy-start.4
  136.4 1.9 %copy-start.43 = (f32[512]{0:T(512)S(1)}, f32[512]{0:T(512)}, u32[]{:S(2)}) copy-start(f32[512]{0:T(512)} %param.11) | copy-start | bytes 6148
Sparse Core Ops, SparseCore 0:
  32.0 26.9 all-gather.1
where the time goes:
time: 158 us; the launch traced here: 157 us
  local copies, waits for them, and re-layouts  52.8 us (33%)
  matrix products  38.1 us (24%)
  blocking collectives  28.5 us (18%)
  between operations  14.5 us (9%)
  waiting for transfers between devices  12.6 us (8%)
  other arithmetic  9 us (6%)
    all_to_all x1, blocking collectives, shards(): lax.all_to_all(stacked, 'uly', split_axis=2, concat_axis=1, tiled=True)  17.8 us
    unnamed x121, local copies, waits for them, and re-layouts  14.7 us
    another operation x9, local copies, waits for them, and re-layouts, shards(): jnp.stack([key_pad[start:start + KEY_BLOCK + col_lead] for start in range...  14.4 us
    all_gather x1, waiting for transfers between devices, shards(): lax.all_gather(jnp.stack([key_local, value_local]), 'ctx', axis=1, tiled=...  12.5 us
    dot_general x1, matrix products, group_logits(): jnp.einsum('ihad,nhard->hinr', shifted, keys_low, preferred_element_type=...  10.9 us
    all_to_all x1, blocking collectives, shards(): lax.all_to_all(attended, 'uly', split_axis=0, concat_axis=1, tiled=True)  10.7 us
    dot_general x1, matrix products, group_logits(): jnp.einsum('ihad,nhard->hinr', shifted, keys_high, preferred_element_type...  10.4 us
    dot_general x1, matrix products, convolved_keys(): jnp.einsum('harc,nchd->nhard', high, key_heads, preferred_element_type=jn...  8.7 us
  transfers between devices with their start and end apart: 2, of which 2 were waited for; matrix products, arithmetic and copies ran while one was open for 8% of the time, Pallas kernels for 0%

commit v1 on v0

--- a/solution.py
+++ b/solution.py
@@ -11,6 +11,29 @@
 KEY_GROUP = 8
 lowest = -1e30
 epsilon = 1e-06
+
+
+def cut_along(x, dim, length):
+    shape = x.shape
+    blocks = x.reshape(*shape[:dim], length, shape[dim] // length, *shape[dim + 1 :])
+    return jnp.moveaxis(blocks, dim, 0)
+
+
+def in_order(pieces, dim):
+    shape = list(pieces.shape[1:])
+    shape[dim] *= pieces.shape[0]
+    return jnp.moveaxis(pieces, 0, dim).reshape(shape)
+
+
+def swapped_with_each(value, axis, split_dim, concat_dim):
+    size, index = (lax.axis_size(axis), lax.axis_index(axis))
+    tiles = cut_along(value, split_dim, size)
+    outs = [tiles[index]]
+    for step in range(1, size):
+        sent = tiles[index ^ step]
+        outs.append(lax.ppermute(sent, axis, [(i, i ^ step) for i in range(size)]))
+    tiles = jnp.stack(outs)[index ^ jnp.arange(size)]
+    return in_order(tiles, concat_dim)
 
 
 def passed_along(shard, axis, by):
@@ -123,9 +146,7 @@
 
 def shards(query_states, key_states, value_states, score_kernel, head_mixing, head_gain):
     stacked = jnp.stack([query_states, key_states, value_states])
-    query_local, key_local, value_local = lax.all_to_all(
-        stacked, "uly", split_axis=2, concat_axis=1, tiled=True
-    )
+    query_local, key_local, value_local = swapped_with_each(stacked, "uly", 2, 1)
     shard_rows = query_local.shape[0]
     width = query_local.shape[1]
     row_lead = QCONV - 1

time: 158 us -> 152 us (0.962)
  blocking collectives: 28.5 us -> 10.7 us
  waiting for transfers between devices: 12.6 us -> 21.2 us
  starting transfers between devices: 1.29 us -> 7.1 us
    all_to_all x1 -> x0, blocking collectives: 17.8 us -> none  [shards(): lax.all_to_all(stacked, 'uly', split_axis=2, concat_axis=1, tiled=True)]
    ppermute x0 -> x3, waiting for transfers between devices: none -> 7.47 us  [swapped_with_each(): outs.append(lax.ppermute(sent, axis, [(i, i ^ step) for i in range(size)]))]
    ppermute x0 -> x3, starting transfers between devices: none -> 5.8 us  [swapped_with_each(): outs.append(lax.ppermute(sent, axis, [(i, i ^ step) for i in range(size)]))]
    unnamed x121 -> x125, local copies, waits for them, and re-layouts: 14.7 us -> 12 us
    another operation x1 -> x4, local copies, waits for them, and re-layouts: 1.36 us -> 3.01 us  [shards(): stacked = jnp.stack([query_states, key_states, value_states])]
  transfers between devices with their start and end apart: 2 -> 5, of which waited for: 2 -> 4; matrix products, arithmetic and copies ran while one was open for 8% -> 9% of each run, Pallas kernels for 0% -> 0%
where the time goes in v1:
time: 152 us
  local copies, waits for them, and re-layouts  51.9 us (34%)
  matrix products  38.1 us (25%)
  waiting for transfers between devices  21.2 us (14%)
  between operations  14.6 us (10%)
  blocking collectives  10.7 us (7%)
  other arithmetic  7.98 us (5%)
  starting transfers between devices  7.1 us (5%)
    another operation x9, local copies, waits for them, and re-layouts, shards(): jnp.stack([key_pad[start:start + KEY_BLOCK + col_lead] for start in range...  14.4 us
    all_gather x1, waiting for transfers between devices, shards(): lax.all_gather(jnp.stack([key_local, value_local]), 'ctx', axis=1, tiled=...  13.6 us
    unnamed x125, local copies, waits for them, and re-layouts  12 us
    dot_general x1, matrix products, group_logits(): jnp.einsum('ihad,nhard->hinr', shifted, keys_low, preferred_element_type=...  10.9 us
    all_to_all x1, blocking collectives, shards(): lax.all_to_all(attended, 'uly', split_axis=0, concat_axis=1, tiled=True)  10.7 us
    dot_general x1, matrix products, group_logits(): jnp.einsum('ihad,nhard->hinr', shifted, keys_high, preferred_element_type...  10.4 us
    dot_general x1, matrix products, convolved_keys(): jnp.einsum('harc,nchd->nhard', high, key_heads, preferred_element_type=jn...  8.7 us
    ppermute x3, waiting for transfers between devices, swapped_with_each(): outs.append(lax.ppermute(sent, axis, [(i, i ^ step) for i in range(size)]))  7.47 us
  transfers between devices with their start and end apart: 5, of which 4 were waited for; matrix products, arithmetic and copies ran while one was open for 9% of the time, Pallas kernels for 0%

profile of v1, /device:TPU:0, one launch (start us, length us, event | category | flops | bytes accessed | tf_op | source)
XLA Modules:
  0.0 151.6 jit_solution(224983315837740233)
XLA Ops:
  6.5 1.0 stack.75
  7.6 1.0 stack.76
  8.6 1.0 stack.77
  9.7 0.9 constant_dynamic-slice_fusion.3
  10.7 5.1 %collective-permute-start.2 = (bf16[3,32,512]{2,1,0:T(8,128)(2,1)S(1)}, bf16[3,32,512]{2,1,0:T(8,128)(2,1)S(1)}, u32[]{:S(2)}, u32[]{:S(2)}) collective-permute-start(bf16[3,32,512]{2,1,0:T(8,128)(2,1)S(1)} %bitcast.149), channel_id=1, source_target_pairs={{0,3},{1,2},{2,1},{3,0},{4,7},{5,6},{6,5},{7,4},{8,11},{9,10},{10,... | collective-permute-start | bytes 294920 | tf_op jit(solution)/shard_map/ppermute | solution.py:34
  15.9 0.6 collective-permute-start
  16.6 2.8 %collective-permute-done.2 = bf16[3,32,512]{2,1,0:T(8,128)(2,1)S(1)} collective-permute-done((bf16[3,32,512]{2,1,0:T(8,128)(2,1)S(1)}, bf16[3,32,512]{2,1,0:T(8,128)(2,1)S(1)}, u32[]{:S(2)}, u32[]{:S(2)}) %collective-permute-start.2) | collective-permute-done | bytes 98336 | tf_op jit(solution)/shard_map/ppermute | solution.py:34
  19.4 4.7 %collective-permute-done.1 = bf16[3,32,512]{2,1,0:T(8,128)(2,1)S(1)} collective-permute-done((bf16[3,32,512]{2,1,0:T(8,128)(2,1)S(1)}, bf16[3,32,512]{2,1,0:T(8,128)(2,1)S(1)}, u32[]{:S(2)}, u32[]{:S(2)}) %collective-permute-start.1) | collective-permute-done | bytes 98336 | tf_op jit(solution)/shard_map/ppermute | solution.py:34
  24.1 0.6 gather_fusion
  24.7 0.8 pad_maximum_fusion.1
  26.1 0.7 copy.177
  26.8 0.6 copy.176
  27.4 0.7 copy.175
  28.1 0.7 copy.174
  28.8 0.7 copy.173
  29.4 0.7 copy.172
  30.1 0.7 copy.171
  30.8 0.7 slice_reduce_fusion.18
  31.6 1.0 slice_reduce_fusion.17
  32.5 0.8 fusion.108
  33.3 1.2 fusion.84
  34.5 1.2 subtract_compare_fusion.5
  35.8 1.3 collective-permute-start.3
  37.1 0.7 concatenate.21
  38.7 0.1 copy.160
  39.4 0.6 concatenate.20
  40.1 13.6 %all-gather.2.cloned.1.call-done = bf16[2,1024,512]{2,1,0:T(8,128)(2,1)} async-done(((bf16[2,128,512]{2,1,0:T(8,128)(2,1)}), bf16[2,1024,512]{2,1,0:T(8,128)(2,1)}) %all-gather.2.cloned.1.call-update) | async-done | bytes 2097168 | tf_op jit(solution)/shard_map/all_gather | solution.py:160
  53.7 1.7 %slice_bitcast_fusion = (bf16[1024,512]{1,0:T(8,128)(2,1)S(1)}, bf16[1,1024,512]{2,1,0:T(8,128)(2,1)S(1)}) fusion(bf16[2,1024,512]{2,1,0:T(8,128)(2,1)} %all-gather.2.cloned.1.call-done), kind=kLoop, calls=%fused_computation.40 | loop fusion | bytes 4194304 | tf_op jit(solution)/shard_map/unstack | solution.py:160
  55.4 0.7 pad_slice_fusion
  56.1 1.6 %stack.91 = bf16[1,138,4,128]{3,2,1,0:T(4,128)(2,1)} reshape(bf16[138,512]{1,0:T(8,128)(2,1)} %pad_slice_fusion) | data formatting | bytes 282624 | tf_op jit(solution)/shard_map/stack | solution.py:165
  57.7 1.6 %copy_dynamic-update-slice_fusion.7 = bf16[8,138,4,128]{3,1,0,2:T(8,128)(2,1)} fusion(bf16[1,138,4,128]{3,2,1,0:T(4,128)(2,1)} %stack.91), kind=kLoop, calls=%fused_computation.139 | loop fusion | bytes 288768
  59.3 2.4 %fusion.128 = (bf16[1,138,512]{2,1,0:T(8,128)(2,1)}, bf16[1,138,512]{2,1,0:T(8,128)(2,1)}, bf16[1,138,512]{2,1,0:T(8,128)(2,1)}, bf16[1,138,512]{2,1,0:T(8,128)(...) fusion(bf16[2,1024,512]{2,1,0:T(8,128)(2,1)} %all-gather.2.cloned.1.call-done), kind=kLoop, calls=%fused_computation.232 | loop fusion | bytes 1978368 | tf_op jit(solution)/shard_map/slice | solution.py:166
  61.7 1.6 %stack.92 = bf16[1,138,4,128]{3,2,1,0:T(4,128)(2,1)} reshape(bf16[1,138,512]{2,1,0:T(8,128)(2,1)} %get-tuple-element.39) | data formatting | bytes 282624 | tf_op jit(solution)/shard_map/stack | solution.py:165
  63.3 1.6 %stack.93 = bf16[1,138,4,128]{3,2,1,0:T(4,128)(2,1)} reshape(bf16[1,138,512]{2,1,0:T(8,128)(2,1)} %get-tuple-element.38) | data formatting | bytes 282624 | tf_op jit(solution)/shard_map/stack | solution.py:165
  64.9 1.6 %stack.94 = bf16[1,138,4,128]{3,2,1,0:T(4,128)(2,1)} reshape(bf16[1,138,512]{2,1,0:T(8,128)(2,1)} %get-tuple-element.37) | data formatting | bytes 282624 | tf_op jit(solution)/shard_map/stack | solution.py:165
  66.5 1.6 %stack.95 = bf16[1,138,4,128]{3,2,1,0:T(4,128)(2,1)} reshape(bf16[1,138,512]{2,1,0:T(8,128)(2,1)} %get-tuple-element.36) | data formatting | bytes 282624 | tf_op jit(solution)/shard_map/stack | solution.py:165
  68.1 1.6 %stack.96 = bf16[1,138,4,128]{3,2,1,0:T(4,128)(2,1)} reshape(bf16[1,138,512]{2,1,0:T(8,128)(2,1)} %get-tuple-element.35) | data formatting | bytes 282624 | tf_op jit(solution)/shard_map/stack | solution.py:165
  69.7 1.6 %stack.97 = bf16[1,138,4,128]{3,2,1,0:T(4,128)(2,1)} reshape(bf16[1,138,512]{2,1,0:T(8,128)(2,1)} %get-tuple-element.34) | data formatting | bytes 282624 | tf_op jit(solution)/shard_map/stack | solution.py:165
  71.3 1.6 %stack.98 = bf16[1,138,4,128]{3,2,1,0:T(4,128)(2,1)} reshape(bf16[1,138,512]{2,1,0:T(8,128)(2,1)} %get-tuple-element.33) | data formatting | bytes 282624 | tf_op jit(solution)/shard_map/stack | solution.py:165
  72.9 1.6 %copy_dynamic-update-slice_fusion.6 = bf16[8,138,4,128]{3,1,0,2:T(8,128)(2,1)} fusion(bf16[8,138,4,128]{3,1,0,2:T(8,128)(2,1)} %copy_dynamic-update-slice_fusion.7, bf16[1,138,4,128]{3,2,1,0:T(4,128)(2,1)} %stack.92), kind=kLoop, calls=%fused_computation.138 | loop fusion | bytes 288768
  74.5 1.6 %copy_dynamic-update-slice_fusion.5 = bf16[8,138,4,128]{3,1,0,2:T(8,128)(2,1)} fusion(bf16[8,138,4,128]{3,1,0,2:T(8,128)(2,1)} %copy_dynamic-update-slice_fusion.6, bf16[1,138,4,128]{3,2,1,0:T(4,128)(2,1)} %stack.93), kind=kLoop, calls=%fused_computation.137 | loop fusion | bytes 288768
  76.1 1.6 %copy_dynamic-update-slice_fusion.4 = bf16[8,138,4,128]{3,1,0,2:T(8,128)(2,1)} fusion(bf16[8,138,4,128]{3,1,0,2:T(8,128)(2,1)} %copy_dynamic-update-slice_fusion.5, bf16[1,138,4,128]{3,2,1,0:T(4,128)(2,1)} %stack.94), kind=kLoop, calls=%fused_computation.136 | loop fusion | bytes 288768
  77.7 1.6 %copy_dynamic-update-slice_fusion.3 = bf16[8,138,4,128]{3,1,0,2:T(8,128)(2,1)} fusion(bf16[8,138,4,128]{3,1,0,2:T(8,128)(2,1)} %copy_dynamic-update-slice_fusion.4, bf16[1,138,4,128]{3,2,1,0:T(4,128)(2,1)} %stack.95), kind=kLoop, calls=%fused_computation.135 | loop fusion | bytes 288768
  79.3 1.6 %copy_dynamic-update-slice_fusion.2 = bf16[8,138,4,128]{3,1,0,2:T(8,128)(2,1)} fusion(bf16[8,138,4,128]{3,1,0,2:T(8,128)(2,1)} %copy_dynamic-update-slice_fusion.3, bf16[1,138,4,128]{3,2,1,0:T(4,128)(2,1)} %stack.96), kind=kLoop, calls=%fused_computation.134 | loop fusion | bytes 288768
  80.9 1.6 %copy_dynamic-update-slice_fusion.1 = bf16[8,138,4,128]{3,1,0,2:T(8,128)(2,1)} fusion(bf16[8,138,4,128]{3,1,0,2:T(8,128)(2,1)} %copy_dynamic-update-slice_fusion.2, bf16[1,138,4,128]{3,2,1,0:T(4,128)(2,1)} %stack.97), kind=kLoop, calls=%fused_computation.133 | loop fusion | bytes 288768
  82.5 1.6 %copy_dynamic-update-slice_fusion = bf16[8,138,4,128]{3,1,0,2:T(8,128)(2,1)} fusion(bf16[8,138,4,128]{3,1,0,2:T(8,128)(2,1)} %copy_dynamic-update-slice_fusion.1, bf16[1,138,4,128]{3,2,1,0:T(4,128)(2,1)} %stack.98), kind=kLoop, calls=%fused_computation.132 | loop fusion | bytes 288768 | tf_op jit(solution)/shard_map/stack | solution.py:165
  84.3 8.7 %fusion.17 = f32[4,8,128,6,128]{4,2,3,1,0:T(8,128)} fusion(bf16[8,138,4,128]{3,1,0,2:T(8,128)(2,1)} %copy_dynamic-update-slice_fusion, f32[4,6]{1,0:T(4,128)S(1)} %bitcast.152, f32[4,6]{1,0:T(4,128)S(1)} %bitcast.154, f32[4,6]{1,0:T(4,128)S(1)} %bitcast.156, f32[4,6]{1,0:T(4,128)S(1)} %bitcast.158, f32[4,6]{1,0:T(4,128)} %bitcast.160, ...), kind=kOutput, calls=%fused_computation.33 | convolution fusion | flops 873732096 | bytes 13908768 | tf_op jit(solution)/shard_map/harc,nchd->nhard/dot_general | solution.py:69
  93.2 6.3 %fusion.15 = f32[4,8,128,6,128]{4,2,3,1,0:T(8,128)} fusion(bf16[8,138,4,128]{3,1,0,2:T(8,128)(2,1)S(1)} %copy-done, f32[4,6]{1,0:T(4,128)S(1)} %bitcast.153, f32[4,6]{1,0:T(4,128)S(1)} %bitcast.155, f32[4,6]{1,0:T(4,128)S(1)} %bitcast.157, f32[4,6]{1,0:T(4,128)S(1)} %bitcast.159, f32[4,6]{1,0:T(4,128)S(1)} %bitcast.161, f32[4,6]{1,0:T(4,128)S(1)} %bitcast.163, ...), kind=kOutput, calls=%fused_computation.31 | convolution fusion | flops 874156032 | bytes 13908768 | tf_op jit(solution)/shard_map/harc,nchd->nhard/dot_general | solution.py:71
  99.5 1.4 copy.151
  101.0 0.1 fusion.130
  101.6 0.2 copy-done.5
  101.8 0.8 fusion.90
  103.2 10.9 %fusion.1 = f32[4,128,8,128,1]{1,3,4,2,0:T(8,128)S(1)} fusion(f32[4,8,128,6,128]{4,2,3,1,0:T(8,128)} %fusion.17, f32[4,8,128,6,128]{4,2,3,1,0:T(8,128)} %fusion.15, bf16[128,4,6,128]{3,0,2,1:T(8,128)(2,1)S(1)} %constant_dynamic-update-slice_fusion.3), kind=kOutput, calls=%fused_computation.4 | convolution fusion | flops 817889280 | bytes 28049408 | tf_op jit(solution)/shard_map/ihad,nhard->hinr/dot_general | solution.py:107
  114.5 10.4 %fusion.85 = (f32[4,128]{1,0:T(4,128)S(1)}, f32[4,128,8,128]{1,3,2,0:T(8,128)S(1)}) fusion(f32[4,128]{1,0:T(4,128)S(1)} %get-tuple-element.78, pred[128,8,128]{0,2,1:T(8,128)(4,1)S(1)} %get-tuple-element.73, f32[4,128]{1,0:T(4,128)S(1)} %get-tuple-element.71, pred[128,8,128]{0,2,1:T(8,128)(4,1)S(1)} %get-tuple-element.74, ...), kind=kOutput, calls=%fused_computation.116 | convolution fusion | flops 821558784 | bytes 30945280 | tf_op jit(solution)/shard_map/ihad,nhard->hinr/dot_general | solution.py:105
  125.0 1.3 exponential_reduce_fusion
  126.3 1.2 fusion.13
  127.8 1.0 copy.192
  128.8 1.0 copy.191
  129.8 1.0 copy.190
  130.8 0.2 copy.189
  131.1 1.8 %multiply_reduce_fusion = (f32[128,4]{0,1:T(4,128)S(1)}, f32[128,4,128]{0,2,1:T(8,128)S(1)}) fusion(bf16[1024,4,128]{0,2,1:T(8,128)(2,1)S(1)} %bitcast.136, f32[128,1024]{1,0:T(8,128)S(1)} %copy-done.3, f32[4]{0:T(128)S(1)} %copy-done.50, f32[128,1024]{1,0:T(8,128)S(1)} %copy-done.4, f32[4]{0:T(128)S(1)} %copy-done.51, f32[128,1024]{1,0:T(8,128)} %copy.190, ...), kind=kOutput, calls=%fused_computation.128 | convolution fusion | flops 138542592 | bytes 3409984 | tf_op jit(solution)/shard_map/hik,khd->ihd/dot_general | solution.py:137
  133.1 0.1 copy.193
  133.3 10.7 %all_to_all.19 = bf16[4,32,512]{2,1,0:T(8,128)(2,1)S(1)} all-to-all(bf16[4,32,512]{2,1,0:T(8,128)(2,1)S(1)} %all_to_all.14), channel_id=1, replica_groups=mesh['ctx'=8,'uly'=4] {'uly'}, dimensions={0} | all-to-all | bytes 262144 | tf_op jit(solution)/shard_map/all_to_all | solution.py:201
  144.1 0.7 copy.208
  (170 shorter events, 4.4 us)
Async XLA Ops:
  6.5 47.2 %all-gather.2.cloned.1.call-start = ((), (), s32[]{:S(2)}) async-start(), calls=%async_computation.1 | async-start | bytes 2359296 | tf_op jit(solution)/shard_map/all_gather | solution.py:160
  10.6 14.9 %copy-start.23 = (f32[4,6,11]{2,0,1:T(4,128)S(1)}, f32[4,6,11]{2,0,1:T(4,128)}, u32[]{:S(2)}) copy-start(f32[4,6,11]{2,0,1:T(4,128)} %param.9) | copy-start | bytes 3172
  10.7 8.7 %collective-permute-start.2 = (bf16[3,32,512]{2,1,0:T(8,128)(2,1)S(1)}, bf16[3,32,512]{2,1,0:T(8,128)(2,1)S(1)}, u32[]{:S(2)}, u32[]{:S(2)}) collective-permute-start(bf16[3,32,512]{2,1,0:T(8,128)(2,1)S(1)} %bitcast.149), channel_id=1, source_target_pairs={{0,3},{1,2},{2,1},{3,0},{4,7},{5,6},{6,5},{7,4},{8,11},{9,10},{10,... | collective-permute-start | bytes 294920 | tf_op jit(solution)/shard_map/ppermute | solution.py:34
  15.8 8.2 %collective-permute-start.1 = (bf16[3,32,512]{2,1,0:T(8,128)(2,1)S(1)}, bf16[3,32,512]{2,1,0:T(8,128)(2,1)S(1)}, u32[]{:S(2)}, u32[]{:S(2)}) collective-permute-start(bf16[3,32,512]{2,1,0:T(8,128)(2,1)S(1)} %bitcast.150), channel_id=1, source_target_pairs={{0,2},{1,3},{2,0},{3,1},{4,6},{5,7},{6,4},{7,5},{8,10},{9,11},{10,... | collective-permute-start | bytes 294920 | tf_op jit(solution)/shard_map/ppermute | solution.py:34
  15.9 14.9 %copy-start.31 = (f32[4,4]{1,0:T(4,128)S(1)}, f32[4,4]{1,0:T(4,128)}, u32[]{:S(2)}) copy-start(f32[4,4]{1,0:T(4,128)} %param.10) | copy-start | bytes 196
  15.9 8.1 %collective-permute-start = (bf16[3,32,512]{2,1,0:T(8,128)(2,1)S(1)}, bf16[3,32,512]{2,1,0:T(8,128)(2,1)S(1)}, u32[]{:S(2)}, u32[]{:S(2)}) collective-permute-start(bf16[3,32,512]{2,1,0:T(8,128)(2,1)S(1)} %bitcast.151), channel_id=1, source_target_pairs={{0,1},{1,0},{2,3},{3,2},{4,5},{5,4},{6,7},{7,6},{8,9},{9,8},{10,11... | collective-permute-start | bytes 294920 | tf_op jit(solution)/shard_map/ppermute | solution.py:34
  35.8 2.1 %collective-permute-start.3 = (bf16[5,512]{1,0:T(8,128)(2,1)S(1)}, bf16[5,512]{1,0:T(8,128)(2,1)S(1)}, u32[]{:S(2)}, u32[]{:S(2)}) collective-permute-start(bf16[5,512]{1,0:T(8,128)(2,1)S(1)} %slice.358), channel_id=1, source_target_pairs={{0,4},{4,8},{8,12},{12,16},{16,20},{20,24},{24,28},{1,5},{5,9},{9,... | collective-permute-start | bytes 15368 | tf_op jit(solution)/shard_map/ppermute | solution.py:42
  84.1 8.9 %copy-start = (bf16[8,138,4,128]{3,1,0,2:T(8,128)(2,1)S(1)}, bf16[8,138,4,128]{3,1,0,2:T(8,128)(2,1)}, u32[]{:S(2)}) copy-start(bf16[8,138,4,128]{3,1,0,2:T(8,128)(2,1)} %copy_dynamic-update-slice_fusion) | copy-start | bytes 3391492
  84.1 8.9 %copy-start.12 = (pred[128,138]{0,1:T(8,128)(4,1)S(1)}, pred[128,138]{0,1:T(8,128)(4,1)}, u32[]{:S(2)}) copy-start(pred[128,138]{0,1:T(8,128)(4,1)} %get-tuple-element.85) | copy-start | bytes 52996
  84.1 8.9 %copy-start.13 = (pred[128,138]{0,1:T(8,128)(4,1)S(1)}, pred[128,138]{0,1:T(8,128)(4,1)}, u32[]{:S(2)}) copy-start(pred[128,138]{0,1:T(8,128)(4,1)} %get-tuple-element.86) | copy-start | bytes 52996
  84.1 8.9 %copy-start.14 = (pred[128,138]{0,1:T(8,128)(4,1)S(1)}, pred[128,138]{0,1:T(8,128)(4,1)}, u32[]{:S(2)}) copy-start(pred[128,138]{0,1:T(8,128)(4,1)} %get-tuple-element.87) | copy-start | bytes 52996
  84.1 8.9 %copy-start.15 = (pred[128,138]{0,1:T(8,128)(4,1)S(1)}, pred[128,138]{0,1:T(8,128)(4,1)}, u32[]{:S(2)}) copy-start(pred[128,138]{0,1:T(8,128)(4,1)} %get-tuple-element.88) | copy-start | bytes 52996
  84.1 8.9 %copy-start.16 = (pred[128,138]{0,1:T(8,128)(4,1)S(1)}, pred[128,138]{0,1:T(8,128)(4,1)}, u32[]{:S(2)}) copy-start(pred[128,138]{0,1:T(8,128)(4,1)} %get-tuple-element.89) | copy-start | bytes 52996
  84.2 8.9 %copy-start.17 = (pred[128,138]{0,1:T(8,128)(4,1)S(1)}, pred[128,138]{0,1:T(8,128)(4,1)}, u32[]{:S(2)}) copy-start(pred[128,138]{0,1:T(8,128)(4,1)} %get-tuple-element.90) | copy-start | bytes 52996
  84.2 8.9 %copy-start.18 = (pred[128,138]{0,1:T(8,128)(4,1)S(1)}, pred[128,138]{0,1:T(8,128)(4,1)}, u32[]{:S(2)}) copy-start(pred[128,138]{0,1:T(8,128)(4,1)} %get-tuple-element.91) | copy-start | bytes 52996
  84.2 8.9 %copy-start.19 = (pred[128,138]{0,1:T(8,128)(4,1)S(1)}, pred[128,138]{0,1:T(8,128)(4,1)}, u32[]{:S(2)}) copy-start(pred[128,138]{0,1:T(8,128)(4,1)} %get-tuple-element.92) | copy-start | bytes 52996
  84.2 8.9 %copy-start.20 = (pred[128,138]{0,1:T(8,128)(4,1)S(1)}, pred[128,138]{0,1:T(8,128)(4,1)}, u32[]{:S(2)}) copy-start(pred[128,138]{0,1:T(8,128)(4,1)} %get-tuple-element.93) | copy-start | bytes 52996
  84.2 8.9 %copy-start.21 = (pred[128,138]{0,1:T(8,128)(4,1)S(1)}, pred[128,138]{0,1:T(8,128)(4,1)}, u32[]{:S(2)}) copy-start(pred[128,138]{0,1:T(8,128)(4,1)} %get-tuple-element.94) | copy-start | bytes 52996
  84.2 8.9 %copy-start.22 = (pred[128,138]{0,1:T(8,128)(4,1)S(1)}, pred[128,138]{0,1:T(8,128)(4,1)}, u32[]{:S(2)}) copy-start(pred[128,138]{0,1:T(8,128)(4,1)} %get-tuple-element.95) | copy-start | bytes 52996
  84.2 8.9 %copy-start.24 = (f32[4,6,1]{1,0,2:T(4,128)S(1)}, f32[4,6,1]{1,0,2:T(4,128)}, u32[]{:S(2)}) copy-start(f32[4,6,1]{1,0,2:T(4,128)} %copy.177) | copy-start | bytes 292
  84.2 8.9 %copy-start.25 = (f32[4,6,1]{1,0,2:T(4,128)S(1)}, f32[4,6,1]{1,0,2:T(4,128)}, u32[]{:S(2)}) copy-start(f32[4,6,1]{1,0,2:T(4,128)} %copy.176) | copy-start | bytes 292
  84.2 8.9 %copy-start.26 = (f32[4,6,1]{1,0,2:T(4,128)S(1)}, f32[4,6,1]{1,0,2:T(4,128)}, u32[]{:S(2)}) copy-start(f32[4,6,1]{1,0,2:T(4,128)} %copy.175) | copy-start | bytes 292
  84.2 8.9 %copy-start.27 = (f32[4,6,1]{1,0,2:T(4,128)S(1)}, f32[4,6,1]{1,0,2:T(4,128)}, u32[]{:S(2)}) copy-start(f32[4,6,1]{1,0,2:T(4,128)} %copy.174) | copy-start | bytes 292
  84.3 8.9 %copy-start.28 = (f32[4,6,1]{1,0,2:T(4,128)S(1)}, f32[4,6,1]{1,0,2:T(4,128)}, u32[]{:S(2)}) copy-start(f32[4,6,1]{1,0,2:T(4,128)} %copy.173) | copy-start | bytes 292
  84.3 8.9 %copy-start.29 = (f32[4,6,1]{1,0,2:T(4,128)S(1)}, f32[4,6,1]{1,0,2:T(4,128)}, u32[]{:S(2)}) copy-start(f32[4,6,1]{1,0,2:T(4,128)} %copy.172) | copy-start | bytes 292
  84.3 8.9 %copy-start.30 = (f32[4,6,1]{1,0,2:T(4,128)S(1)}, f32[4,6,1]{1,0,2:T(4,128)}, u32[]{:S(2)}) copy-start(f32[4,6,1]{1,0,2:T(4,128)} %copy.171) | copy-start | bytes 292
  100.9 0.9 copy-start.5
  100.9 0.9 copy-start.32
  103.1 11.0 %copy-start.33 = (f32[4]{0:T(128)S(1)}, f32[4]{0:T(128)}, u32[]{:S(2)}) copy-start(f32[4]{0:T(128)} %get-tuple-element.11) | copy-start | bytes 52
  103.1 11.0 %copy-start.34 = (f32[4]{0:T(128)S(1)}, f32[4]{0:T(128)}, u32[]{:S(2)}) copy-start(f32[4]{0:T(128)} %get-tuple-element.12) | copy-start | bytes 52
  103.1 11.0 %copy-start.35 = (f32[4]{0:T(128)S(1)}, f32[4]{0:T(128)}, u32[]{:S(2)}) copy-start(f32[4]{0:T(128)} %get-tuple-element.13) | copy-start | bytes 52
  103.1 11.0 %copy-start.36 = (f32[4]{0:T(128)S(1)}, f32[4]{0:T(128)}, u32[]{:S(2)}) copy-start(f32[4]{0:T(128)} %get-tuple-element.16) | copy-start | bytes 52
  103.1 11.0 %copy-start.37 = (f32[4]{0:T(128)S(1)}, f32[4]{0:T(128)}, u32[]{:S(2)}) copy-start(f32[4]{0:T(128)} %get-tuple-element.17) | copy-start | bytes 52
  103.1 11.0 %copy-start.38 = (f32[4]{0:T(128)S(1)}, f32[4]{0:T(128)}, u32[]{:S(2)}) copy-start(f32[4]{0:T(128)} %get-tuple-element.20) | copy-start | bytes 52
  103.1 11.1 %copy-start.39 = (f32[4]{0:T(128)S(1)}, f32[4]{0:T(128)}, u32[]{:S(2)}) copy-start(f32[4]{0:T(128)} %get-tuple-element.15) | copy-start | bytes 52
  103.1 11.1 %copy-start.40 = (f32[4]{0:T(128)S(1)}, f32[4]{0:T(128)}, u32[]{:S(2)}) copy-start(f32[4]{0:T(128)} %get-tuple-element.19) | copy-start | bytes 52
  103.2 11.1 %copy-start.41 = (f32[4]{0:T(128)S(1)}, f32[4]{0:T(128)}, u32[]{:S(2)}) copy-start(f32[4]{0:T(128)} %get-tuple-element.22) | copy-start | bytes 52
  103.2 11.1 %copy-start.42 = (f32[4]{0:T(128)S(1)}, f32[4]{0:T(128)}, u32[]{:S(2)}) copy-start(f32[4]{0:T(128)} %get-tuple-element.24) | copy-start | bytes 52
  103.2 11.2 %copy-start.44 = (f32[4]{0:T(128)S(1)}, f32[4]{0:T(128)}, u32[]{:S(2)}) copy-start(f32[4]{0:T(128)} %get-tuple-element.10) | copy-start | bytes 52
  103.2 11.2 %copy-start.45 = (f32[4]{0:T(128)S(1)}, f32[4]{0:T(128)}, u32[]{:S(2)}) copy-start(f32[4]{0:T(128)} %get-tuple-element.14) | copy-start | bytes 52
  103.2 11.2 %copy-start.46 = (f32[4]{0:T(128)S(1)}, f32[4]{0:T(128)}, u32[]{:S(2)}) copy-start(f32[4]{0:T(128)} %get-tuple-element.18) | copy-start | bytes 52
  103.2 11.2 %copy-start.47 = (f32[4]{0:T(128)S(1)}, f32[4]{0:T(128)}, u32[]{:S(2)}) copy-start(f32[4]{0:T(128)} %get-tuple-element.21) | copy-start | bytes 52
  103.2 11.2 %copy-start.48 = (f32[4]{0:T(128)S(1)}, f32[4]{0:T(128)}, u32[]{:S(2)}) copy-start(f32[4]{0:T(128)} %get-tuple-element.23) | copy-start | bytes 52
  103.2 11.3 %copy-start.1 = (pred[128,8,128]{0,2,1:T(8,128)(4,1)S(1)}, pred[128,8,128]{0,2,1:T(8,128)(4,1)}, u32[]{:S(2)}) copy-start(pred[128,8,128]{0,2,1:T(8,128)(4,1)} %get-tuple-element.77) | copy-start | bytes 393220
  125.0 1.3 copy-start.6
  125.0 1.3 copy-start.7
  125.0 1.3 copy-start.8
  125.0 1.3 copy-start.9
  125.0 1.3 copy-start.10
  125.0 1.3 copy-start.11
  127.7 3.3 %copy-start.2 = (bf16[1,1024,512]{1,2,0:T(8,128)(2,1)S(1)}, bf16[1,1024,512]{1,2,0:T(8,128)(2,1)}, u32[]{:S(2)}) copy-start(bf16[1,1024,512]{1,2,0:T(8,128)(2,1)} %copy.151) | copy-start | bytes 3145732
  127.7 3.3 %copy-start.49 = (f32[4]{0:T(128)S(1)}, f32[4]{0:T(128)}, u32[]{:S(2)}) copy-start(f32[4]{0:T(128)} %get-tuple-element.25) | copy-start | bytes 52
  127.7 3.3 %copy-start.50 = (f32[4]{0:T(128)S(1)}, f32[4]{0:T(128)}, u32[]{:S(2)}) copy-start(f32[4]{0:T(128)} %get-tuple-element.26) | copy-start | bytes 52
  127.8 3.3 %copy-start.51 = (f32[4]{0:T(128)S(1)}, f32[4]{0:T(128)}, u32[]{:S(2)}) copy-start(f32[4]{0:T(128)} %get-tuple-element.27) | copy-start | bytes 52
  127.8 3.3 %copy-start.52 = (f32[4]{0:T(128)S(1)}, f32[4]{0:T(128)}, u32[]{:S(2)}) copy-start(f32[4]{0:T(128)} %get-tuple-element.28) | copy-start | bytes 52
  128.8 2.3 %copy-start.3 = (f32[128,1024]{1,0:T(8,128)S(1)}, f32[128,1024]{1,0:T(8,128)}, u32[]{:S(2)}) copy-start(f32[128,1024]{1,0:T(8,128)} %copy.192) | copy-start | bytes 1572868
  129.8 1.3 copy-start.4
  131.1 1.9 %copy-start.43 = (f32[512]{0:T(512)S(1)}, f32[512]{0:T(512)}, u32[]{:S(2)}) copy-start(f32[512]{0:T(512)} %param.11) | copy-start | bytes 6148
Sparse Core Ops, SparseCore 0:
  25.6 28.0 all-gather.1
